TPU v7x, 256 devices: a whole 4x4x8 slice. The times are simulated.
256 devices in a mesh: grp: 32 (over x, z), shard: 8 (over y, core).
Axes of the slice: x: 4, y: 4, z: 8, core: 2. Of those that a mesh axis runs over, the one named last changes fastest.
Arguments:
- layer_inputs: bfloat16 [131072, 1600], P(('grp', 'shard')), may hold values from -6 to 6
- cotangents: bfloat16 [131072, 1600], P(('grp', 'shard')), may hold values from -0.25 to 0.25
- weight: bfloat16 [1600, 1600], P('shard'), may hold values from -0.15625 to 0.15625
- error_state: float32 [32, 1600, 1600], P('grp', 'shard'), may hold values from -6 to 6
- momentum: float32 [1600, 1600], P('shard'), may hold values from -0.75 to 0.75
- bias_momentum: float32 [1600], replicated, may hold values from -6 to 6
- start_basis: float32 [1600, 32], replicated, may hold values from -6 to 6
- next_inputs: bfloat16 [131072, 1600], P(('grp', 'shard')), may hold values from -6 to 6
Outputs:
- next_outputs: bfloat16 [131072, 1600], P(('grp', 'shard'))
- new_error: float32 [32, 1600, 1600], P('grp', 'shard')
- new_momentum: float32 [1600, 1600], P('shard')
- new_bias_momentum: float32 [1600], replicated
All inputs are finite; a program needn't handle non-finite values.
Results may differ from a plain program's by a relative error of at most 0.015.
Values may be sent and summed in bfloat16 or wider, within the bound.
No kernel may reach another device: no remote copies, remote signals or barrier semaphores. Data moves between devices by JAX's collectives and lax.ppermute only.
A program may use at most 128 MiB of HBM per device.

v0:
```python
import jax
import jax.numpy as jnp
from jax import lax
from jax.sharding import PartitionSpec as P

momentum_decay = 0.9
learn_rate = 0.1


def shards(
    layer_inputs, cotangents, weight, error_state, momentum, bias_momentum, start_basis, next_inputs
):
    highest = lax.Precision.HIGHEST
    group_count = lax.axis_size("grp")
    columns = layer_inputs
    gradient = lax.psum_scatter(
        lax.dot_general(
            columns, cotangents, (((0,), (0,)), ((), ())), preferred_element_type=jnp.float32
        ).astype(jnp.bfloat16),
        "shard",
        scatter_dimension=0,
        tiled=True,
    ).astype(jnp.float32)
    column_sums = lax.psum(jnp.sum(cotangents, axis=0, dtype=jnp.float32), ("grp", "shard"))
    corrected = gradient + error_state[0]
    basis = start_basis
    ortho = start_basis
    for round_index in range(2):
        local_factor = jnp.dot(corrected, basis, precision=highest)
        own_rows = lax.psum(local_factor, "grp")
        gram = lax.psum(jnp.dot(own_rows.T, own_rows, precision=highest), "shard")
        lower_factor = jnp.linalg.cholesky(gram)
        ortho = jax.scipy.linalg.solve_triangular(lower_factor, own_rows.T, lower=True).T
        partial_basis = lax.dot_general(
            corrected, ortho, (((0,), (0,)), ((), ())), precision=highest
        )
        summed = lax.psum(partial_basis, ("grp", "shard"))
        basis = summed / group_count
    approx = jnp.dot(ortho, basis.T, precision=highest)
    new_error = (corrected - approx)[None, :, :]
    new_momentum = momentum_decay * momentum + approx
    new_bias_momentum = momentum_decay * bias_momentum + column_sums / group_count
    new_weight = (weight.astype(jnp.float32) - learn_rate * new_momentum).astype(jnp.bfloat16)
    columns = next_inputs
    projected = jnp.dot(
        columns,
        lax.all_gather(new_weight, "shard", axis=0, tiled=True),
        preferred_element_type=jnp.float32,
    )
    return (projected.astype(jnp.bfloat16), new_error, new_momentum, new_bias_momentum)


def solution(mesh):
    placed = (
        P(("grp", "shard"), None),
        P(("grp", "shard"), None),
        P("shard", None),
        P("grp", "shard", None),
        P("shard", None),
        P(),
        P(),
        P(("grp", "shard"), None),
    )
    return jax.shard_map(
        shards,
        mesh=mesh,
        in_specs=placed,
        out_specs=(P(("grp", "shard"), None), P("grp", "shard", None), P("shard", None), P()),
        check_vma=False,
    )
```

profile of v0, /device:TPU:1, one launch (start us, length us, event | category | flops | bytes accessed | tf_op | source)
XLA Modules:
  0.0 1017.4 jit_solution(5363052511592432300)
XLA Ops:
  7.2 1.4 copy-done
  8.6 6.3 convolution_convert_fusion
  15.0 50.3 %reduce-scatter.4.cloned.1.call-done = bf16[200,1600]{1,0:T(8,128)(2,1)} async-done(((bf16[1600,1600]{1,0:T(8,128)(2,1)}), bf16[200,1600]{1,0:T(8,128)(2,1)}) %reduce-scatter.4.cloned.1.call-update) | async-done | bytes 640016
  65.3 2.4 fusion.23
  67.8 115.4 %psum.49 = f32[200,32]{0,1:T(8,128)S(1)} all-reduce(f32[200,32]{0,1:T(8,128)S(1)} %fusion.23), channel_id=1, replica_groups=mesh['grp'=32,'shard'=8] {'grp'}, use_global_device_ids=true, to_apply=%region_1.0 | all-reduce | flops 6400 | bytes 51200 | tf_op jit(solution)/shard_map/psum | solution.py:30
  183.2 0.2 fusion.26
  183.4 51.6 %psum.50 = f32[32,32]{0,1:T(8,128)S(1)} all-reduce(f32[32,32]{0,1:T(8,128)S(1)} %fusion.26), channel_id=1, replica_groups=mesh['grp'=32,'shard'=8] {'shard'}, use_global_device_ids=true, to_apply=%region_2.0 | all-reduce | flops 1024 | bytes 8192 | tf_op jit(solution)/shard_map/psum | solution.py:31
  234.9 0.1 copy.17
  235.0 2.9 cholesky.44
  238.0 0.6 compare_reduce_fusion.1
  238.6 0.7 fusion.11
  239.3 2.4 custom-call.6
  241.7 0.2 fusion.9
  242.0 4.8 fusion.22
  246.8 248.4 %all-reduce.4.cloned.1.call-done = f32[1600,32]{1,0:T(8,128)} async-done(((f32[1600,32]{1,0:T(8,128)}), f32[1600,32]{1,0:T(8,128)}) %all-reduce.4.cloned.1.call-update) | async-done | bytes 204816 | tf_op jit(solution)/shard_map/psum | solution.py:37
  495.2 2.9 fusion.3
  498.1 114.1 %psum.52 = f32[200,32]{0,1:T(8,128)S(1)} all-reduce(f32[200,32]{0,1:T(8,128)S(1)} %fusion.3), channel_id=1, replica_groups=mesh['grp'=32,'shard'=8] {'grp'}, use_global_device_ids=true, to_apply=%region_6.0 | all-reduce | flops 6400 | bytes 51200 | tf_op jit(solution)/shard_map/psum | solution.py:30
  612.2 0.2 fusion.27
  612.4 46.1 %psum.53 = f32[32,32]{0,1:T(8,128)S(1)} all-reduce(f32[32,32]{0,1:T(8,128)S(1)} %fusion.27), channel_id=1, replica_groups=mesh['grp'=32,'shard'=8] {'shard'}, use_global_device_ids=true, to_apply=%region_7.0 | all-reduce | flops 1024 | bytes 8192 | tf_op jit(solution)/shard_map/psum | solution.py:31
  658.5 0.1 copy.19
  658.6 2.9 cholesky.55
  661.6 0.6 compare_reduce_fusion
  662.2 0.7 fusion.12
  662.9 2.4 custom-call.7
  665.3 0.2 fusion.7
  665.5 4.8 fusion.21
  670.4 248.4 %all-reduce.6.cloned.1.call-done = f32[1600,32]{1,0:T(8,128)} async-done(((f32[1600,32]{1,0:T(8,128)}), f32[1600,32]{1,0:T(8,128)}) %all-reduce.6.cloned.1.call-update) | async-done | bytes 204816 | tf_op jit(solution)/shard_map/psum | solution.py:37
  918.8 5.3 subtract_convert_fusion
  924.1 1.7 convert_reduce_fusion
  925.8 77.1 %psum.55 = f32[1600]{0:T(1024)S(1)} all-reduce(f32[1600]{0:T(1024)S(1)} %convert_reduce_fusion), channel_id=1, replica_groups=mesh['grp'=32,'shard'=8] {'grp','shard'}, use_global_device_ids=true, to_apply=%region_10.13 | all-reduce | flops 1600 | bytes 12800 | tf_op jit(solution)/shard_map/psum | solution.py:24
  1002.9 0.6 multiply_add_fusion.1
  1003.5 7.4 fusion
  (20 shorter events, 0.3 us)
Async XLA Ops:
  7.2 1.4 copy-start
  7.2 58.1 %reduce-scatter.4.cloned.1.call-start = ((), (), s32[]{:S(2)}) async-start(), calls=%async_computation.4 | async-start | bytes 5990400
  14.9 50.4 %copy-start.1 = (f32[1,200,1600]{2,1,0:T(8,128)S(1)}, f32[1,200,1600]{2,1,0:T(8,128)}, u32[]{:S(2)}) copy-start(f32[1,200,1600]{2,1,0:T(8,128)} %param.14) | copy-start | bytes 3840004
  14.9 50.4 %copy-start.2 = (f32[1600,32]{0,1:T(8,128)S(1)}, f32[1600,32]{0,1:T(8,128)}, u32[]{:S(2)}) copy-start(f32[1600,32]{0,1:T(8,128)} %param.17) | copy-start | bytes 614404
  15.0 480.3 %all-reduce.4.cloned.1.call-start = ((), (), s32[]{:S(2)}) async-start(), calls=%async_computation.1 | async-start | bytes 1638400 | tf_op jit(solution)/shard_map/psum | solution.py:37
  246.8 672.0 %all-reduce.6.cloned.1.call-start = ((), (), s32[]{:S(2)}) async-start(), calls=%async_computation.2 | async-start | bytes 1638400 | tf_op jit(solution)/shard_map/psum | solution.py:37
  670.4 333.1 %all-gather.2.cloned.1.call-start = ((), (), s32[]{:S(2)}) async-start(), calls=%async_computation.3 | async-start | bytes 5990400 | tf_op jit(solution)/shard_map/all_gather | solution.py:47
  924.0 78.8 %copy-start.3 = (f32[1600]{0:T(1024)S(1)}, f32[1600]{0:T(1024)}, u32[]{:S(2)}) copy-start(f32[1600]{0:T(1024)} %param.16) | copy-start | bytes 19204
Sparse Core Ops, SparseCore 0:
  15.1 50.1 reduce-scatter.3
  246.9 248.2 all-reduce.3
  670.5 248.2 all-reduce.5
  924.2 38.9 all-gather.1
where the time goes:
time: 1020 us
  waiting for transfers between devices  547 us (54%)
  blocking collectives  404 us (40%)
  matrix products  34.6 us (3%)
  other arithmetic  15.7 us (2%)
  between operations  13.8 us (1%)
    psum x2, waiting for transfers between devices, shards(): summed = lax.psum(partial_basis, ('grp', 'shard'))  497 us
    psum x2, blocking collectives, shards(): own_rows = lax.psum(local_factor, 'grp')  230 us
    psum x2, blocking collectives, shards(): gram = lax.psum(jnp.dot(own_rows.T, own_rows, precision=highest), 'shard')  97.7 us
    psum x1, blocking collectives, shards(): lax.psum(jnp.sum(cotangents, axis=0, dtype=jnp.float32), ('grp', 'shard'))  77.1 us
    unnamed x5, waiting for transfers between devices  50.4 us
  transfers between devices with their start and end apart: 4, of which 3 were waited for; matrix products, arithmetic and copies ran while one was open for 0% of the time, Pallas kernels for 0%

commit v1 on v0

--- a/solution.py
+++ b/solution.py
@@ -34,7 +34,8 @@
         partial_basis = lax.dot_general(
             corrected, ortho, (((0,), (0,)), ((), ())), precision=highest
         )
-        summed = lax.psum(partial_basis, ("grp", "shard"))
+        odd = lax.all_gather(partial_basis, axis_name=("grp", "shard"))
+        summed = jnp.sum(odd, 0)
         basis = summed / group_count
     approx = jnp.dot(ortho, basis.T, precision=highest)
     new_error = (corrected - approx)[None, :, :]

time: 1020 us -> 914 us (0.90)
  waiting for transfers between devices: 547 us -> 416 us
  other arithmetic: 15.7 us -> 50.5 us
    psum x2 -> x0, waiting for transfers between devices: 497 us -> none  [shards(): summed = lax.psum(partial_basis, ('grp', 'shard'))]
    all_gather x0 -> x2, waiting for transfers between devices: none -> 366 us  [shards(): odd = lax.all_gather(partial_basis, axis_name=('grp', 'shard'))]
    reduce_sum x0 -> x2, other arithmetic: none -> 34.7 us  [shards(): summed = jnp.sum(odd, 0)]
where the time goes in v1:
time: 914 us; the launch traced here: 913 us
  waiting for transfers between devices  416 us (46%)
  blocking collectives  404 us (44%)
  other arithmetic  50.5 us (6%)
  matrix products  26.4 us (3%)
  between operations  13.9 us (2%)
    all_gather x2, waiting for transfers between devices, shards(): odd = lax.all_gather(partial_basis, axis_name=('grp', 'shard'))  366 us
    psum x2, blocking collectives, shards(): own_rows = lax.psum(local_factor, 'grp')  229 us
    psum x2, blocking collectives, shards(): gram = lax.psum(jnp.dot(own_rows.T, own_rows, precision=highest), 'shard')  99.7 us
    psum x1, blocking collectives, shards(): lax.psum(jnp.sum(cotangents, axis=0, dtype=jnp.float32), ('grp', 'shard'))  75.8 us
    unnamed x5, waiting for transfers between devices  50.5 us
    reduce_sum x2, other arithmetic, shards(): summed = jnp.sum(odd, 0)  34.7 us
  transfers between devices with their start and end apart: 4, of which 3 were waited for; matrix products, arithmetic and copies ran while one was open for 0% of the time, Pallas kernels for 0%

profile of v1, /device:TPU:1, one launch (start us, length us, event | category | flops | bytes accessed | tf_op | source)
XLA Modules:
  0.0 913.3 jit_solution(6676171794267850291)
XLA Ops:
  7.2 1.4 copy-done
  8.6 6.3 convolution_convert_fusion
  15.0 50.4 %reduce-scatter.4.cloned.1.call-done = bf16[200,1600]{1,0:T(8,128)(2,1)} async-done(((bf16[1600,1600]{1,0:T(8,128)(2,1)}), bf16[200,1600]{1,0:T(8,128)(2,1)}) %reduce-scatter.4.cloned.1.call-update) | async-done | bytes 640016
  65.4 2.5 fusion.21
  67.9 115.0 %psum.35 = f32[200,32]{0,1:T(8,128)S(1)} all-reduce(f32[200,32]{0,1:T(8,128)S(1)} %fusion.21), channel_id=1, replica_groups=mesh['grp'=32,'shard'=8] {'grp'}, use_global_device_ids=true, to_apply=%region_1.0 | all-reduce | flops 6400 | bytes 51200 | tf_op jit(solution)/shard_map/psum | solution.py:30
  183.1 52.0 %psum.36 = f32[32,32]{0,1:T(8,128)S(1)} all-reduce(f32[32,32]{0,1:T(8,128)S(1)} %fusion.24), channel_id=1, replica_groups=mesh['grp'=32,'shard'=8] {'shard'}, use_global_device_ids=true, to_apply=%region_2.0 | all-reduce | flops 1024 | bytes 8192 | tf_op jit(solution)/shard_map/psum | solution.py:31
  235.2 2.9 cholesky.44
  238.2 0.6 compare_reduce_fusion.1
  238.8 0.7 fusion.11
  239.5 2.4 custom-call.6
  241.9 0.2 fusion.9
  242.2 1.7 convolution_bitcast_fusion.1
  243.9 182.8 %all-gather.10.cloned.1.call-done = f32[256,1600,32]{1,2,0:T(8,128)} async-done(((f32[1,1600,32]{1,2,0:T(8,128)}), f32[256,1600,32]{1,2,0:T(8,128)}) %all-gather.10.cloned.1.call-update) | async-done | bytes 52428816 | tf_op jit(solution)/shard_map/all_gather | solution.py:37
  426.7 17.4 %reduce_sum.27 = f32[1600,32]{0,1:T(8,128)S(1)} reduce(f32[256,1600,32]{1,2,0:T(8,128)} %all-gather.10.cloned.1.call-done, f32[]{:T(128)} %constant.41.clone.1), dimensions={0}, to_apply=%region_5.0 | reduce | flops 13056000 | bytes 52633604 | tf_op jit(solution)/shard_map/reduce_sum | solution.py:38
  444.1 1.4 fusion.3
  445.5 113.7 %psum.37 = f32[200,32]{0,1:T(8,128)S(1)} all-reduce(f32[200,32]{0,1:T(8,128)S(1)} %fusion.3), channel_id=1, replica_groups=mesh['grp'=32,'shard'=8] {'grp'}, use_global_device_ids=true, to_apply=%region_6.0 | all-reduce | flops 6400 | bytes 51200 | tf_op jit(solution)/shard_map/psum | solution.py:30
  559.2 0.2 fusion.25
  559.4 47.7 %psum.38 = f32[32,32]{0,1:T(8,128)S(1)} all-reduce(f32[32,32]{0,1:T(8,128)S(1)} %fusion.25), channel_id=1, replica_groups=mesh['grp'=32,'shard'=8] {'shard'}, use_global_device_ids=true, to_apply=%region_7.0 | all-reduce | flops 1024 | bytes 8192 | tf_op jit(solution)/shard_map/psum | solution.py:31
  607.1 2.9 cholesky.55
  610.1 0.6 compare_reduce_fusion
  610.7 0.7 fusion.12
  611.4 2.4 custom-call.7
  613.8 0.2 fusion.7
  614.1 0.6 copy-done.5
  614.7 1.7 convolution_bitcast_fusion
  616.5 182.8 %all-gather.12.cloned.1.call-done = f32[256,1600,32]{1,2,0:T(8,128)} async-done(((f32[1,1600,32]{1,2,0:T(8,128)}), f32[256,1600,32]{1,2,0:T(8,128)}) %all-gather.12.cloned.1.call-update) | async-done | bytes 52428816 | tf_op jit(solution)/shard_map/all_gather | solution.py:37
  799.3 17.4 %reduce_sum.28 = f32[1600,32]{0,1:T(8,128)S(1)} reduce(f32[256,1600,32]{1,2,0:T(8,128)} %all-gather.12.cloned.1.call-done, f32[]{:T(128)} %constant.41.clone.1), dimensions={0}, to_apply=%region_8.0 | reduce | flops 13056000 | bytes 52633604 | tf_op jit(solution)/shard_map/reduce_sum | solution.py:38
  816.6 4.4 subtract_convert_fusion
  821.1 1.7 convert_reduce_fusion
  822.8 75.8 %psum.39 = f32[1600]{0:T(1024)S(1)} all-reduce(f32[1600]{0:T(1024)S(1)} %convert_reduce_fusion), channel_id=1, replica_groups=mesh['grp'=32,'shard'=8] {'grp','shard'}, use_global_device_ids=true, to_apply=%region_10.13 | all-reduce | flops 1600 | bytes 12800 | tf_op jit(solution)/shard_map/psum | solution.py:24
  898.7 0.6 multiply_add_fusion.1
  899.3 7.5 fusion
  (30 shorter events, 0.6 us)
Async XLA Ops:
  7.2 1.4 copy-start
  7.2 58.2 %reduce-scatter.4.cloned.1.call-start = ((), (), s32[]{:S(2)}) async-start(), calls=%async_computation.4 | async-start | bytes 5990400
  14.9 50.5 %copy-start.2 = (f32[1,200,1600]{2,1,0:T(8,128)S(1)}, f32[1,200,1600]{2,1,0:T(8,128)}, u32[]{:S(2)}) copy-start(f32[1,200,1600]{2,1,0:T(8,128)} %param.14) | copy-start | bytes 3840004
  14.9 50.5 %copy-start.6 = (f32[1600,32]{0,1:T(8,128)S(1)}, f32[1600,32]{0,1:T(8,128)}, u32[]{:S(2)}) copy-start(f32[1600,32]{0,1:T(8,128)} %param.17) | copy-start | bytes 614404
  15.0 411.8 %all-gather.10.cloned.1.call-start = ((), (), s32[]{:S(2)}) async-start(), calls=%async_computation.2 | async-start | bytes 54738944 | tf_op jit(solution)/shard_map/all_gather | solution.py:37
  65.4 176.7 %copy-start.3 = (bf16[200,1600]{1,0:T(8,128)(2,1)S(1)}, bf16[200,1600]{1,0:T(8,128)(2,1)}, u32[]{:S(2)}) copy-start(bf16[200,1600]{1,0:T(8,128)(2,1)} %reduce-scatter.4.cloned.1.call-done) | copy-start | bytes 1920004
  243.9 555.4 %all-gather.12.cloned.1.call-start = ((), (), s32[]{:S(2)}) async-start(), calls=%async_computation.3 | async-start | bytes 54738944 | tf_op jit(solution)/shard_map/all_gather | solution.py:37
  614.1 0.6 copy-start.5
  616.4 200.2 %copy-start.4 = (f32[200,1600]{1,0:T(8,128)S(1)}, f32[200,1600]{1,0:T(8,128)}, u32[]{:S(2)}) copy-start(f32[200,1600]{1,0:T(8,128)} %param.15) | copy-start | bytes 3840004
  616.4 282.8 %all-gather.8.cloned.1.call-start = ((), (), s32[]{:S(2)}) async-start(), calls=%async_computation.1 | async-start | bytes 5990400 | tf_op jit(solution)/shard_map/all_gather | solution.py:48
  821.0 77.6 %copy-start.7 = (f32[1600]{0:T(1024)S(1)}, f32[1600]{0:T(1024)}, u32[]{:S(2)}) copy-start(f32[1600]{0:T(1024)} %param.16) | copy-start | bytes 19204
  899.3 7.5 copy-start.1
Sparse Core Ops, SparseCore 0:
  15.1 50.2 reduce-scatter.3
  244.0 182.6 all-gather.9
  616.5 182.6 all-gather.11
  821.2 36.8 all-gather.7
